TPU v7x, 256 devices: a whole 4x4x8 slice. The times are simulated.
256 devices in a mesh: link: 64 (over x, z, core), col: 4 (over y).
Axes of the slice: x: 4, y: 4, z: 8, core: 2. Of those that a mesh axis runs over, the one named last changes fastest.
Arguments:
- values: bfloat16 [1024, 16, 128], P('link'), may hold values from -6 to 6
- tiles: int32 [1024, 16], P('link'), may hold values from 0 to 127, all different within a row
- barrier: float32 [1024], P('link'), may hold values from 0.5 to 2
- slack: float32 [16384], replicated, may hold values from 0.5 to 2
- order: int32 [128], replicated, may hold values from 0 to 127, each once
Outputs:
- factored: float32 [16384, 16384], P('link', 'col')
Inputs may be any that keep to these rules, and one draw needn't show every extreme that they name: `tiles`: each commodity's 16 tile numbers are distinct, and every tile is named by some commodity. `order`: each tile number appears once.
All inputs are finite; a program needn't handle non-finite values.
Results may differ from a plain program's by a relative error of at most 0.0038.
Values may be sent and summed in bfloat16 or wider, within the bound.
No kernel may reach another device: no remote copies, remote signals or barrier semaphores. Data moves between devices by JAX's collectives and lax.ppermute only.
A program may use at most 64 MiB of HBM per device.

v0:
```python
import jax
import jax.numpy as jnp
from jax import lax
from jax.sharding import PartitionSpec as P

PANEL = 128


def spread(value, axis, source):
    kept = jnp.where(lax.axis_index(axis) == source, value, 0).astype(value.dtype)
    return lax.psum(kept, axis)


def densify(tile_vals, tile_ids, targets):
    onehot = (tile_ids[:, :, None] == targets[None, None, :]).astype(jnp.bfloat16)
    dense_out = jnp.einsum("kjp,kju->kpu", onehot, tile_vals, preferred_element_type=jnp.float32)
    dense_out = dense_out.astype(jnp.bfloat16)
    return dense_out.reshape(tile_vals.shape[0], targets.shape[0] * tile_vals.shape[2])


def contract_rows(left_side, right_side):
    return lax.dot_general(
        left_side, right_side, (((0,), (0,)), ((), ())), preferred_element_type=jnp.float32
    )


def local(values, tiles, barrier, slack, order):
    link_devs = lax.axis_size("link")
    col_devs = lax.axis_size("col")
    link_idx = lax.axis_index("link")
    col_idx = lax.axis_index("col")
    link_count = slack.shape[0]
    rows_dev = link_count // link_devs
    cols_dev = link_count // col_devs
    tile_len = values.shape[2]
    ntiles = order.shape[0]
    factor = link_count / (values.shape[0] * link_devs * values.shape[1] * tile_len)
    scaled = (jnp.sqrt(barrier * factor)[:, None, None] * values.astype(jnp.float32)).astype(
        jnp.bfloat16
    )
    own_dense = densify(scaled, tiles, order)
    link_rows = lax.all_to_all(own_dense, "link", split_axis=1, concat_axis=0, tiled=True)
    col_slab = lax.dynamic_slice_in_dim(own_dense, col_idx * cols_dev, cols_dev, 1)
    normal = contract_rows(link_rows, lax.all_gather(col_slab, "link", axis=0, tiled=True))
    rows_g = link_idx * rows_dev + jnp.arange(rows_dev)
    cols_g = col_idx * cols_dev + jnp.arange(cols_dev)
    perm_hot = (order[:, None] == jnp.arange(ntiles)[None, :]).astype(jnp.float32)
    slack_ord = jnp.dot(
        perm_hot, slack.reshape(ntiles, tile_len), precision=lax.Precision.HIGHEST
    ).reshape(link_count)
    slack_rows = lax.dynamic_slice_in_dim(slack_ord, link_idx * rows_dev, rows_dev)
    matrix = normal + jnp.where(
        rows_g[:, None] == cols_g[None, :], slack_rows[:, None], jnp.float32(0.0)
    )
    panels = []
    for panel_no in range(2):
        first_col = panel_no * PANEL
        diag_block = matrix[first_col : first_col + PANEL, first_col : first_col + PANEL]
        factor_local = jnp.linalg.cholesky(diag_block)
        lower_fac = spread(factor_local, "link", 0)
        solved = jax.scipy.linalg.solve_triangular(
            lower_fac, matrix[:, first_col : first_col + PANEL].T, lower=True
        ).T
        picker = ((rows_g - first_col)[:, None] == jnp.arange(PANEL)[None, :]).astype(jnp.float32)
        diag_rows = jnp.dot(picker, lower_fac, precision=lax.Precision.HIGHEST)
        column = jnp.where(
            rows_g[:, None] < first_col,
            jnp.float32(0.0),
            jnp.where(rows_g[:, None] < first_col + PANEL, diag_rows, solved),
        )
        across = spread(column.astype(jnp.bfloat16), "col", 0)
        everyone = lax.all_gather(across, "link", axis=0, tiled=True)
        col_part = lax.dynamic_slice_in_dim(everyone, col_idx * cols_dev, cols_dev, 0)
        matrix = matrix - lax.dot_general(
            across, col_part, (((1,), (1,)), ((), ())), preferred_element_type=jnp.float32
        )
        panels.append(column)
    panel_block = jnp.concatenate(panels, 1)
    padded = jnp.pad(panel_block, ((0, 0), (0, cols_dev - 2 * PANEL)))
    return jnp.where(
        cols_g[None, :] < 2 * PANEL,
        padded,
        jnp.where(rows_g[:, None] < 2 * PANEL, jnp.float32(0.0), matrix),
    )


def solution(mesh):
    in_specs = (P("link", None, None), P("link", None), P("link"), P(), P())
    out_specs = P("link", "col")
    return jax.shard_map(local, mesh=mesh, in_specs=in_specs, out_specs=out_specs, check_vma=False)
```

profile of v0, /device:TPU:1, one launch (start us, length us, event | category | flops | bytes accessed | tf_op | source)
XLA Modules:
  0.0 768.8 jit_solution(11925922518593524493)
XLA Ops:
  6.5 0.7 multiply_sqrt_fusion
  7.2 1.4 convolution_convert_fusion
  9.9 1.1 copy.12
  10.9 13.0 %all-to-all-start = ((bf16[16,64,256]{2,0,1:T(8,128)(2,1)}), bf16[16,64,256]{2,0,1:T(8,128)(2,1)S(1)}, u32[]{:S(2)}, u32[]{:S(2)}) async-start(bf16[16,64,256]{2,0,1:T(8,128)(2,1)} %copy.12), calls=%async_computation | async-start | bytes 1048576 | tf_op jit(solution)/shard_map/all_to_all | solution.py:42
  24.3 19.3 %all-to-all-done = bf16[16,64,256]{2,0,1:T(8,128)(2,1)S(1)} async-done(((bf16[16,64,256]{2,0,1:T(8,128)(2,1)}), bf16[16,64,256]{2,0,1:T(8,128)(2,1)S(1)}, u32[]{:S(2)}, u32[]{:S(2)}) %all-to-all-start) | async-done | bytes 524320 | tf_op jit(solution)/shard_map/all_to_all | solution.py:42
  43.6 54.6 %all-gather.4.cloned.1.call-done = bf16[1024,4096]{1,0:T(8,128)(2,1)} async-done(((bf16[16,4096]{1,0:T(8,128)(2,1)}), bf16[1024,4096]{1,0:T(8,128)(2,1)}) %all-gather.4.cloned.1.call-update) | async-done | bytes 8388624 | tf_op jit(solution)/shard_map/all_gather | solution.py:44
  98.2 6.6 convolution_add_fusion
  104.8 2.0 copy-done.1
  106.9 0.9 fusion.14
  107.8 11.7 %cholesky.44 = f32[128,128]{1,0:T(8,128)S(1)} custom-call(f32[128,128]{1,0:T(8,128)S(1)} %fusion.14), custom_call_target="Cholesky" | custom-call | tf_op jit(solution)/shard_map/jit(cholesky)/cholesky | solution.py:59
  120.2 1.3 select_select_fusion.1
  121.6 167.5 %all-reduce.6.cloned.1.call-done = f32[128,128]{1,0:T(8,128)} async-done(((f32[128,128]{1,0:T(8,128)}), f32[128,128]{1,0:T(8,128)}) %all-reduce.6.cloned.1.call-update) | async-done | bytes 65552 | tf_op jit(solution)/shard_map/psum | solution.py:11
  289.1 0.8 select_bitcast_fusion.1
  289.9 9.8 %custom-call.6 = f32[1,128,128]{1,2,0:T(8,128)S(1)} custom-call(f32[1,128,128]{2,1,0:T(8,128)S(1)} %select_bitcast_fusion.1), custom_call_target="InvertDiagBlocksLowerTriangular" | custom-call | tf_op jit(solution)/shard_map/jit(_solve_triangular)/triangular_solve | solution.py:61
  299.7 1.1 fusion.8
  300.9 1.9 convert_select_fusion.1
  302.8 41.2 %all-reduce.8.cloned.1.call-done = bf16[256,128]{0,1:T(8,128)(2,1)} async-done(((bf16[256,128]{0,1:T(8,128)(2,1)}), bf16[256,128]{0,1:T(8,128)(2,1)}) %all-reduce.8.cloned.1.call-update) | async-done | bytes 65552 | tf_op jit(solution)/shard_map/psum | solution.py:11
  344.3 81.0 %all-gather.6.cloned.1.call-done = bf16[16384,128]{0,1:T(8,128)(2,1)} async-done(((bf16[256,128]{0,1:T(8,128)(2,1)}), bf16[16384,128]{0,1:T(8,128)(2,1)}) %all-gather.6.cloned.1.call-update) | async-done | bytes 4194320 | tf_op jit(solution)/shard_map/all_gather | solution.py:72
  425.2 3.3 convolution_subtract_fusion.1
  428.6 2.0 copy-done.2
  430.7 0.9 fusion.12
  431.5 11.7 %cholesky.55 = f32[128,128]{1,0:T(8,128)S(1)} custom-call(f32[128,128]{1,0:T(8,128)S(1)} %fusion.12), custom_call_target="Cholesky" | custom-call | tf_op jit(solution)/shard_map/jit(cholesky)/cholesky | solution.py:59
  443.9 1.3 select_select_fusion
  445.3 170.2 %all-reduce.10.cloned.1.call-done = f32[128,128]{1,0:T(8,128)} async-done(((f32[128,128]{1,0:T(8,128)}), f32[128,128]{1,0:T(8,128)}) %all-reduce.10.cloned.1.call-update) | async-done | bytes 65552 | tf_op jit(solution)/shard_map/psum | solution.py:11
  615.4 0.8 select_bitcast_fusion
  616.3 9.8 %custom-call.7 = f32[1,128,128]{1,2,0:T(8,128)S(1)} custom-call(f32[1,128,128]{2,1,0:T(8,128)S(1)} %select_bitcast_fusion), custom_call_target="InvertDiagBlocksLowerTriangular" | custom-call | tf_op jit(solution)/shard_map/jit(_solve_triangular)/triangular_solve | solution.py:61
  626.1 1.1 fusion.9
  627.3 1.9 convert_select_fusion
  629.2 41.2 %all-reduce.12.cloned.1.call-done = bf16[256,128]{0,1:T(8,128)(2,1)} async-done(((bf16[256,128]{0,1:T(8,128)(2,1)}), bf16[256,128]{0,1:T(8,128)(2,1)}) %all-reduce.12.cloned.1.call-update) | async-done | bytes 65552 | tf_op jit(solution)/shard_map/psum | solution.py:11
  670.4 81.4 %all-gather.8.cloned.1.call-done = bf16[16384,128]{0,1:T(8,128)(2,1)} async-done(((bf16[256,128]{0,1:T(8,128)(2,1)}), bf16[16384,128]{0,1:T(8,128)(2,1)}) %all-gather.8.cloned.1.call-update) | async-done | bytes 4194320 | tf_op jit(solution)/shard_map/all_gather | solution.py:72
  751.8 4.6 fusion.1
  756.3 5.6 copy.18
  (39 shorter events, 3.7 us)
Async XLA Ops:
  6.5 17.5 %copy-start = (f32[16384]{0:T(1024)S(1)}, f32[16384]{0:T(1024)}, u32[]{:S(2)}) copy-start(f32[16384]{0:T(1024)} %param.11) | copy-start | bytes 196612
  6.5 17.5 %copy-start.3 = (s32[128]{0:T(128)S(1)}, s32[128]{0:T(128)}, u32[]{:S(2)}) copy-start(s32[128]{0:T(128)} %param.12) | copy-start | bytes 1540
  6.5 91.6 %all-gather.4.cloned.1.call-start = ((), (), s32[]{:S(2)}) async-start(), calls=%async_computation.1 | async-start | bytes 8519680 | tf_op jit(solution)/shard_map/all_gather | solution.py:44
  10.9 32.7 %all-to-all-start = ((bf16[16,64,256]{2,0,1:T(8,128)(2,1)}), bf16[16,64,256]{2,0,1:T(8,128)(2,1)S(1)}, u32[]{:S(2)}, u32[]{:S(2)}) async-start(bf16[16,64,256]{2,0,1:T(8,128)(2,1)} %copy.12), calls=%async_computation | async-start | bytes 1048576 | tf_op jit(solution)/shard_map/all_to_all | solution.py:42
  23.9 265.1 %all-reduce.6.cloned.1.call-start = ((), (), s32[]{:S(2)}) async-start(), calls=%async_computation.2 | async-start | bytes 131072 | tf_op jit(solution)/shard_map/psum | solution.py:11
  104.8 2.0 copy-start.1
  121.5 222.5 %all-reduce.8.cloned.1.call-start = ((), (), s32[]{:S(2)}) async-start(), calls=%async_computation.3 | async-start | bytes 131072 | tf_op jit(solution)/shard_map/psum | solution.py:11
  302.8 122.5 %all-gather.6.cloned.1.call-start = ((), (), s32[]{:S(2)}) async-start(), calls=%async_computation.4 | async-start | bytes 4259840 | tf_op jit(solution)/shard_map/all_gather | solution.py:72
  344.0 271.4 %all-reduce.10.cloned.1.call-start = ((), (), s32[]{:S(2)}) async-start(), calls=%async_computation.5 | async-start | bytes 131072 | tf_op jit(solution)/shard_map/psum | solution.py:11
  428.5 2.0 copy-start.2
  445.2 225.1 %all-reduce.12.cloned.1.call-start = ((), (), s32[]{:S(2)}) async-start(), calls=%async_computation.6 | async-start | bytes 131072 | tf_op jit(solution)/shard_map/psum | solution.py:11
  629.1 122.6 %all-gather.8.cloned.1.call-start = ((), (), s32[]{:S(2)}) async-start(), calls=%async_computation.7 | async-start | bytes 4259840 | tf_op jit(solution)/shard_map/all_gather | solution.py:72
Sparse Core Ops, SparseCore 0:
  10.1 88.0 all-gather.3
  121.6 167.4 all-reduce.5
  302.9 41.0 all-reduce.7
  346.4 78.8 all-gather.5
  445.3 170.0 all-reduce.9
  629.3 41.0 all-reduce.11
  672.9 78.8 all-gather.7
where the time goes:
time: 769 us
  waiting for transfers between devices  656 us (85%)
  other arithmetic  51.1 us (7%)
  matrix products  22.1 us (3%)
  between operations  13.7 us (2%)
  starting transfers between devices  13.4 us (2%)
  local copies, waits for them, and re-layouts  12.1 us (2%)
    psum x4, waiting for transfers between devices, spread(): return lax.psum(kept, axis)  420 us
    all_gather x2, waiting for transfers between devices, local(): everyone = lax.all_gather(across, 'link', axis=0, tiled=True)  162 us
    all_gather x1, waiting for transfers between devices, local(): lax.all_gather(col_slab, 'link', axis=0, tiled=True)  54.6 us
    another operation x6, other arithmetic, local(): factor_local = jnp.linalg.cholesky(diag_block)  24.8 us
    another operation x4, other arithmetic, local(): jax.scipy.linalg.solve_triangular(lower_fac, matrix[:, first_col:first_co...  21.3 us
    all_to_all x1, waiting for transfers between devices, local(): lax.all_to_all(own_dense, 'link', split_axis=1, concat_axis=0, tiled=True)  19.3 us
  transfers between devices with their start and end apart: 8, of which 8 were waited for; matrix products, arithmetic and copies ran while one was open for 0% of the time, Pallas kernels for 0%

commit v1 on v0

--- a/solution.py
+++ b/solution.py
@@ -4,6 +4,14 @@
 from jax.sharding import PartitionSpec as P
 
 PANEL = 128
+
+
+def search_copies(page, named_axis):
+    step_out = jnp.concatenate(
+        lax.all_to_all(jnp.stack([page] * lax.axis_size(named_axis), axis=0), named_axis, 0, 0),
+        axis=0,
+    )
+    return step_out
 
 
 def spread(value, axis, source):
@@ -69,7 +77,7 @@
             jnp.where(rows_g[:, None] < first_col + PANEL, diag_rows, solved),
         )
         across = spread(column.astype(jnp.bfloat16), "col", 0)
-        everyone = lax.all_gather(across, "link", axis=0, tiled=True)
+        everyone = search_copies(across, "link")
         col_part = lax.dynamic_slice_in_dim(everyone, col_idx * cols_dev, cols_dev, 0)
         matrix = matrix - lax.dot_general(
             across, col_part, (((1,), (1,)), ((), ())), preferred_element_type=jnp.float32

time: 769 us -> 829 us (1.078)
  waiting for transfers between devices: 656 us -> 682 us
  starting transfers between devices: 13.4 us -> 39.1 us
    all_to_all x0 -> x2, waiting for transfers between devices: none -> 192 us  [search_copies(): lax.all_to_all(jnp.stack([page] * lax.axis_size(named_axis), axis=0), nam...]
    all_gather x2 -> x0, waiting for transfers between devices: 162 us -> none  [local(): everyone = lax.all_gather(across, 'link', axis=0, tiled=True)]
    all_to_all x0 -> x2, starting transfers between devices: none -> 26 us  [search_copies(): lax.all_to_all(jnp.stack([page] * lax.axis_size(named_axis), axis=0), nam...]
where the time goes in v1:
time: 829 us; the launch traced here: 828 us
  waiting for transfers between devices  682 us (82%)
  other arithmetic  51.1 us (6%)
  starting transfers between devices  39.1 us (5%)
  matrix products  21.9 us (3%)
  local copies, waits for them, and re-layouts  20 us (2%)
  between operations  13.4 us (2%)
    psum x4, waiting for transfers between devices, spread(): return lax.psum(kept, axis)  416 us
    all_to_all x2, waiting for transfers between devices, search_copies(): lax.all_to_all(jnp.stack([page] * lax.axis_size(named_axis), axis=0), nam...  192 us
    all_gather x1, waiting for transfers between devices, local(): lax.all_gather(col_slab, 'link', axis=0, tiled=True)  54.6 us
    all_to_all x2, starting transfers between devices, search_copies(): lax.all_to_all(jnp.stack([page] * lax.axis_size(named_axis), axis=0), nam...  26 us
    another operation x6, other arithmetic, local(): factor_local = jnp.linalg.cholesky(diag_block)  24.8 us
    another operation x4, other arithmetic, local(): jax.scipy.linalg.solve_triangular(lower_fac, matrix[:, first_col:first_co...  21.3 us
    all_to_all x1, waiting for transfers between devices, local(): lax.all_to_all(own_dense, 'link', split_axis=1, concat_axis=0, tiled=True)  19.3 us
  transfers between devices with their start and end apart: 8, of which 8 were waited for; matrix products, arithmetic and copies ran while one was open for 0% of the time, Pallas kernels for 0%

profile of v1, /device:TPU:1, one launch (start us, length us, event | category | flops | bytes accessed | tf_op | source)
XLA Modules:
  0.0 827.5 jit_solution(10599890348467425141)
XLA Ops:
  7.2 1.4 convolution_convert_fusion
  9.9 1.1 copy.14
  10.9 13.0 %all-to-all-start = ((bf16[16,64,256]{2,0,1:T(8,128)(2,1)}), bf16[16,64,256]{2,0,1:T(8,128)(2,1)S(1)}, u32[]{:S(2)}, u32[]{:S(2)}) async-start(bf16[16,64,256]{2,0,1:T(8,128)(2,1)} %copy.14), calls=%async_computation | async-start | bytes 1048576 | tf_op jit(solution)/shard_map/all_to_all | solution.py:50
  24.3 19.3 %all-to-all-done = bf16[16,64,256]{2,0,1:T(8,128)(2,1)S(1)} async-done(((bf16[16,64,256]{2,0,1:T(8,128)(2,1)}), bf16[16,64,256]{2,0,1:T(8,128)(2,1)S(1)}, u32[]{:S(2)}, u32[]{:S(2)}) %all-to-all-start) | async-done | bytes 524320 | tf_op jit(solution)/shard_map/all_to_all | solution.py:50
  43.6 54.6 %all-gather.2.cloned.1.call-done = bf16[1024,4096]{1,0:T(8,128)(2,1)} async-done(((bf16[16,4096]{1,0:T(8,128)(2,1)}), bf16[1024,4096]{1,0:T(8,128)(2,1)}) %all-gather.2.cloned.1.call-update) | async-done | bytes 8388624 | tf_op jit(solution)/shard_map/all_gather | solution.py:52
  98.2 6.6 convolution_add_fusion
  104.8 2.0 copy-done.1
  107.8 11.7 %cholesky.44 = f32[128,128]{1,0:T(8,128)S(1)} custom-call(f32[128,128]{1,0:T(8,128)S(1)} %fusion.14), custom_call_target="Cholesky" | custom-call | tf_op jit(solution)/shard_map/jit(cholesky)/cholesky | solution.py:67
  120.2 1.3 select_select_fusion.1
  121.6 167.5 %all-reduce.6.cloned.1.call-done = f32[128,128]{1,0:T(8,128)} async-done(((f32[128,128]{1,0:T(8,128)}), f32[128,128]{1,0:T(8,128)}) %all-reduce.6.cloned.1.call-update) | async-done | bytes 65552 | tf_op jit(solution)/shard_map/psum | solution.py:19
  289.9 9.8 %custom-call.6 = f32[1,128,128]{1,2,0:T(8,128)S(1)} custom-call(f32[1,128,128]{2,1,0:T(8,128)S(1)} %select_bitcast_fusion.1), custom_call_target="InvertDiagBlocksLowerTriangular" | custom-call | tf_op jit(solution)/shard_map/jit(_solve_triangular)/triangular_solve | solution.py:69
  299.7 1.1 fusion.8
  300.9 1.9 convert_select_fusion.1
  302.8 41.2 %all-reduce.8.cloned.1.call-done = bf16[256,128]{0,1:T(8,128)(2,1)} async-done(((bf16[256,128]{0,1:T(8,128)(2,1)}), bf16[256,128]{0,1:T(8,128)(2,1)}) %all-reduce.8.cloned.1.call-update) | async-done | bytes 65552 | tf_op jit(solution)/shard_map/psum | solution.py:19
  344.0 0.9 copy.17
  344.9 3.0 stack.4
  347.9 13.0 %all-to-all-start.1 = ((bf16[64,256,128]{2,1,0:T(8,128)(2,1)}), bf16[64,256,128]{2,1,0:T(8,128)(2,1)}, u32[]{:S(2)}, u32[]{:S(2)}) async-start(bf16[64,256,128]{2,1,0:T(8,128)(2,1)} %stack.4), calls=%async_computation.1 | async-start | bytes 8388608 | tf_op jit(solution)/shard_map/all_to_all | solution.py:11
  361.0 95.8 %all-to-all-done.1 = bf16[64,256,128]{2,1,0:T(8,128)(2,1)} async-done(((bf16[64,256,128]{2,1,0:T(8,128)(2,1)}), bf16[64,256,128]{2,1,0:T(8,128)(2,1)}, u32[]{:S(2)}, u32[]{:S(2)}) %all-to-all-start.1) | async-done | bytes 4194336 | tf_op jit(solution)/shard_map/all_to_all | solution.py:11
  456.8 3.2 convolution_subtract_fusion.1
  460.0 2.0 copy-done.2
  463.0 11.7 %cholesky.55 = f32[128,128]{1,0:T(8,128)S(1)} custom-call(f32[128,128]{1,0:T(8,128)S(1)} %fusion.12), custom_call_target="Cholesky" | custom-call | tf_op jit(solution)/shard_map/jit(cholesky)/cholesky | solution.py:67
  475.4 1.3 select_select_fusion
  476.7 166.5 %all-reduce.10.cloned.1.call-done = f32[128,128]{1,0:T(8,128)} async-done(((f32[128,128]{1,0:T(8,128)}), f32[128,128]{1,0:T(8,128)}) %all-reduce.10.cloned.1.call-update) | async-done | bytes 65552 | tf_op jit(solution)/shard_map/psum | solution.py:19
  644.1 9.8 %custom-call.7 = f32[1,128,128]{1,2,0:T(8,128)S(1)} custom-call(f32[1,128,128]{2,1,0:T(8,128)S(1)} %select_bitcast_fusion), custom_call_target="InvertDiagBlocksLowerTriangular" | custom-call | tf_op jit(solution)/shard_map/jit(_solve_triangular)/triangular_solve | solution.py:69
  653.9 1.1 fusion.9
  655.0 1.9 convert_select_fusion
  656.9 41.2 %all-reduce.12.cloned.1.call-done = bf16[256,128]{0,1:T(8,128)(2,1)} async-done(((bf16[256,128]{0,1:T(8,128)(2,1)}), bf16[256,128]{0,1:T(8,128)(2,1)}) %all-reduce.12.cloned.1.call-update) | async-done | bytes 65552 | tf_op jit(solution)/shard_map/psum | solution.py:19
  699.1 3.0 stack.5
  702.1 13.0 %all-to-all-start.2 = ((bf16[64,256,128]{2,1,0:T(8,128)(2,1)}), bf16[64,256,128]{2,1,0:T(8,128)(2,1)}, u32[]{:S(2)}, u32[]{:S(2)}) async-start(bf16[64,256,128]{2,1,0:T(8,128)(2,1)} %stack.5), calls=%async_computation.2 | async-start | bytes 8388608 | tf_op jit(solution)/shard_map/all_to_all | solution.py:11
  715.1 95.8 %all-to-all-done.2 = bf16[64,256,128]{2,1,0:T(8,128)(2,1)} async-done(((bf16[64,256,128]{2,1,0:T(8,128)(2,1)}), bf16[64,256,128]{2,1,0:T(8,128)(2,1)}, u32[]{:S(2)}, u32[]{:S(2)}) %all-to-all-start.2) | async-done | bytes 4194336 | tf_op jit(solution)/shard_map/all_to_all | solution.py:11
  810.9 4.4 fusion.1
  815.4 5.6 copy.22
  (45 shorter events, 8.4 us)
Async XLA Ops:
  6.5 17.5 %copy-start = (f32[16384]{0:T(1024)S(1)}, f32[16384]{0:T(1024)}, u32[]{:S(2)}) copy-start(f32[16384]{0:T(1024)} %param.11) | copy-start | bytes 196612
  6.5 17.5 %copy-start.5 = (s32[128]{0:T(128)S(1)}, s32[128]{0:T(128)}, u32[]{:S(2)}) copy-start(s32[128]{0:T(128)} %param.12) | copy-start | bytes 1540
  6.5 91.6 %all-gather.2.cloned.1.call-start = ((), (), s32[]{:S(2)}) async-start(), calls=%async_computation.3 | async-start | bytes 8519680 | tf_op jit(solution)/shard_map/all_gather | solution.py:52
  10.9 32.7 %all-to-all-start = ((bf16[16,64,256]{2,0,1:T(8,128)(2,1)}), bf16[16,64,256]{2,0,1:T(8,128)(2,1)S(1)}, u32[]{:S(2)}, u32[]{:S(2)}) async-start(bf16[16,64,256]{2,0,1:T(8,128)(2,1)} %copy.14), calls=%async_computation | async-start | bytes 1048576 | tf_op jit(solution)/shard_map/all_to_all | solution.py:50
  23.9 265.1 %all-reduce.6.cloned.1.call-start = ((), (), s32[]{:S(2)}) async-start(), calls=%async_computation.4 | async-start | bytes 131072 | tf_op jit(solution)/shard_map/psum | solution.py:19
  104.8 2.0 copy-start.1
  121.5 222.5 %all-reduce.8.cloned.1.call-start = ((), (), s32[]{:S(2)}) async-start(), calls=%async_computation.5 | async-start | bytes 131072 | tf_op jit(solution)/shard_map/psum | solution.py:19
  347.9 108.8 %copy-start.3 = (bf16[256,128]{0,1:T(8,128)(2,1)S(1)}, bf16[256,128]{0,1:T(8,128)(2,1)}, u32[]{:S(2)}) copy-start(bf16[256,128]{0,1:T(8,128)(2,1)} %all-reduce.8.cloned.1.call-done) | copy-start | bytes 196612
  347.9 108.8 %all-to-all-start.1 = ((bf16[64,256,128]{2,1,0:T(8,128)(2,1)}), bf16[64,256,128]{2,1,0:T(8,128)(2,1)}, u32[]{:S(2)}, u32[]{:S(2)}) async-start(bf16[64,256,128]{2,1,0:T(8,128)(2,1)} %stack.4), calls=%async_computation.1 | async-start | bytes 8388608 | tf_op jit(solution)/shard_map/all_to_all | solution.py:11
  360.9 282.3 %all-reduce.10.cloned.1.call-start = ((), (), s32[]{:S(2)}) async-start(), calls=%async_computation.6 | async-start | bytes 131072 | tf_op jit(solution)/shard_map/psum | solution.py:19
  460.0 2.0 copy-start.2
  476.7 221.5 %all-reduce.12.cloned.1.call-start = ((), (), s32[]{:S(2)}) async-start(), calls=%async_computation.7 | async-start | bytes 131072 | tf_op jit(solution)/shard_map/psum | solution.py:19
  702.1 108.8 %copy-start.4 = (bf16[256,128]{0,1:T(8,128)(2,1)S(1)}, bf16[256,128]{0,1:T(8,128)(2,1)}, u32[]{:S(2)}) copy-start(bf16[256,128]{0,1:T(8,128)(2,1)} %all-reduce.12.cloned.1.call-done) | copy-start | bytes 196612
  702.1 108.8 %all-to-all-start.2 = ((bf16[64,256,128]{2,1,0:T(8,128)(2,1)}), bf16[64,256,128]{2,1,0:T(8,128)(2,1)}, u32[]{:S(2)}, u32[]{:S(2)}) async-start(bf16[64,256,128]{2,1,0:T(8,128)(2,1)} %stack.5), calls=%async_computation.2 | async-start | bytes 8388608 | tf_op jit(solution)/shard_map/all_to_all | solution.py:11
Sparse Core Ops, SparseCore 0:
  10.1 88.0 all-gather.1
  121.6 167.4 all-reduce.5
  302.9 41.0 all-reduce.7
  476.8 166.3 all-reduce.9
  657.0 41.0 all-reduce.11
